TPU v7x, 32 devices: a whole 2x2x4 slice. The times are simulated.
32 devices in a mesh: grp: 4 (over y, core), blk: 8 (over z, x).
Axes of the slice: x: 2, y: 2, z: 4, core: 2. Of those that a mesh axis runs over, the one named last changes fastest.
Arguments:
- fields: float32 [14, 512, 4096], P(None, 'grp', 'blk'), may hold values from -6 to 6
- react_rate: float32 [512, 4096], P('grp', 'blk'), may hold values from 0.05 to 0.8
- mix_matrix: float32 [14, 14], replicated, may hold values from -1.5 to 1.5
- activation: float32 [14], replicated, may hold values from 0.3 to 4
- inlet_ids: int32 [4, 4096], P(None, 'blk'), may hold values from 0 to 4095
- inlet_weights: float32 [4, 4096], P(None, 'blk'), may hold values from 0.1 to 0.45
- outlet_ids: int32 [4, 4096], P(None, 'blk'), may hold values from 0 to 4095
- outlet_weights: float32 [4, 4096], P(None, 'blk'), may hold values from 0.1 to 0.45
Outputs:
- advanced: float32 [14, 512, 4096], P(None, 'grp', 'blk')
Inputs may be any that keep to these rules, and one draw needn't show every extreme that they name: Every inlet_ids entry names a row of the combustor exit plane. Every outlet_ids entry names a row of the turbine inlet plane.
All inputs are finite; a program needn't handle non-finite values.
Results may differ from a plain program's by a relative error of at most 0.00005.
Values sent between devices are 32-bit elements; how exact they have to be, the bound alone decides.
No kernel may reach another device: no remote copies, remote signals or barrier semaphores. Data moves between devices by JAX's collectives and lax.ppermute only.
A program may use at most 128 MiB of HBM per device.

v0:
```python
import jax
import jax.numpy as jnp
from jax import lax
from jax.sharding import PartitionSpec as P

courant = 0.5
diffusion = 0.1
source_step = 0.5


def padded(cells, sides, width, closed):
    for axis, dim in sides:
        count = lax.axis_size(axis)
        ends = count if closed else count - 1
        head = lax.slice_in_dim(cells, 0, width, axis=dim)
        tail = lax.slice_in_dim(cells, cells.shape[dim] - width, cells.shape[dim], axis=dim)
        cells = jnp.concatenate(
            [
                lax.ppermute(tail, axis, [(i, (i + 1) % count) for i in range(ends)]),
                cells,
                lax.ppermute(head, axis, [((i + 1) % count, i) for i in range(ends)]),
            ],
            axis=dim,
        )
    return cells


def tendency(values, backward, forward, cycle_left, cycle_right, rates, mix_matrix, activation):
    heat = 1.0 + jax.nn.softplus(values[4])
    reaction = rates[None] * values * jnp.exp(-activation[:, None, None] / heat[None])
    source = jnp.einsum("fg,gxr->fxr", mix_matrix, reaction, precision=lax.Precision.HIGHEST)
    advect = -courant * (values - backward)
    spread = diffusion * (backward + forward + cycle_left + cycle_right - 4.0 * values)
    return advect + spread + source_step * source


def faces(values):
    axial_pad = padded(values, (("grp", 1),), 1, False)
    cycle_pad = padded(values, (("blk", 2),), 1, True)
    return (axial_pad, cycle_pad)


def shards(
    fields, react_rate, mix_matrix, activation, inlet_ids, inlet_weights, outlet_ids, outlet_weights
):
    group_count = lax.axis_size("grp")
    group_index = lax.axis_index("grp")
    at_turbine = group_index == group_count - 1
    at_exit = group_index == group_count - 2
    axial_pad, cycle_pad = faces(fields)
    low_row = axial_pad[:, 0, :]
    high_row = axial_pad[:, -1, :]
    donors = lax.all_gather(low_row, "blk", axis=1, tiled=True)
    row_count = donors.shape[1]
    inside = (inlet_ids >= 0) & (inlet_ids < row_count)
    picked = jnp.take(donors, jnp.clip(inlet_ids, 0, row_count - 1), axis=1)
    weight = jnp.where(inside, inlet_weights, 0.0)
    inlet_values = jnp.sum(picked * weight[None], axis=1)
    pressure = lax.all_gather(high_row[4], "blk", axis=0, tiled=True)
    back_pressure = jnp.sum(jnp.take(pressure, outlet_ids) * outlet_weights, axis=0)

    def rate_of(values, axial_pad, cycle_pad):
        last_layer = values[:, -1, :]
        exit_ghost = last_layer.at[4].set(back_pressure)
        low_ghost = jnp.where(at_turbine, inlet_values, axial_pad[:, 0, :])
        high_ghost = jnp.where(
            at_turbine, last_layer, jnp.where(at_exit, exit_ghost, axial_pad[:, -1, :])
        )
        backward = jnp.concatenate([low_ghost[:, None, :], values[:, :-1, :]], axis=1)
        forward = jnp.concatenate([values[:, 1:, :], high_ghost[:, None, :]], axis=1)
        return tendency(
            values,
            backward,
            forward,
            cycle_pad[:, :, :-2],
            cycle_pad[:, :, 2:],
            react_rate,
            mix_matrix,
            activation,
        )

    first_section = fields + rate_of(fields, axial_pad, cycle_pad)
    second_axial, second_cycle = faces(first_section)
    return 0.5 * (fields + first_section + rate_of(first_section, second_axial, second_cycle))


def solution(mesh):
    in_specs = (
        P(None, "grp", "blk"),
        P("grp", "blk"),
        P(),
        P(),
        P(None, "blk"),
        P(None, "blk"),
        P(None, "blk"),
        P(None, "blk"),
    )
    out_specs = P(None, "grp", "blk")
    return jax.shard_map(shards, mesh=mesh, in_specs=in_specs, out_specs=out_specs, check_vma=False)
```

profile of v0, /device:TPU:1, one launch (start us, length us, event | category | flops | bytes accessed | tf_op | source)
XLA Modules:
  0.0 159.8 jit_solution(1495912322812927714)
XLA Ops:
  0.0 1.8 %fusion.48 = (f32[14,128,1]{2,1,0:T(8,128)S(1)}, f32[14,128,1]{2,1,0:T(8,128)S(1)}) fusion(f32[14,128,512]{2,1,0:T(8,128)} %param.12), kind=kLoop, calls=%fused_computation.72 | loop fusion | bytes 28672 | tf_op jit(solution)/shard_map/slice | solution.py:16
  2.1 5.1 %collective-permute-start.3 = (f32[14,128,1]{1,2,0:T(1,128)S(1)}, f32[14,128,1]{1,2,0:T(1,128)S(1)}, u32[]{:S(2)}, u32[]{:S(2)}) collective-permute-start(f32[14,128,1]{1,2,0:T(1,128)S(1)} %copy.67), channel_id=1, source_target_pairs={{1,0},{2,1},{3,2},{4,3},{5,4},{6,5},{7,6},{0,7},{9,8},{10,9},{11,1... | collective-permute-start | bytes 21512 | tf_op jit(solution)/shard_map/ppermute | solution.py:21
  7.5 4.2 %copy.58 = f32[14,128,512]{2,0,1:T(8,128)S(1)} copy(f32[14,128,512]{2,1,0:T(8,128)} %param.12) | data formatting | bytes 7340032 | tf_op args[0]
  11.8 4.0 %collective-permute-start = (f32[14,1,512]{2,0,1:T(8,128)S(1)}, f32[14,1,512]{2,0,1:T(8,128)S(1)}, u32[]{:S(2)}, u32[]{:S(2)}) collective-permute-start(f32[14,1,512]{2,0,1:T(8,128)S(1)} %get-tuple-element.36), channel_id=1, source_target_pairs={{0,8},{8,16},{16,24},{1,9},{9,17},{17,25},{2,10},{10,18},{18,26},{... | collective-permute-start | bytes 86024 | tf_op jit(solution)/shard_map/ppermute | solution.py:19
  15.8 1.9 %collective-permute-start.1 = (f32[14,1,512]{2,0,1:T(8,128)S(1)}, f32[14,1,512]{2,0,1:T(8,128)S(1)}, u32[]{:S(2)}, u32[]{:S(2)}) collective-permute-start(f32[14,1,512]{2,0,1:T(8,128)S(1)} %get-tuple-element.38), channel_id=1, source_target_pairs={{8,0},{16,8},{24,16},{9,1},{17,9},{25,17},{10,2},{18,10},{26,18},{... | collective-permute-start | bytes 86024 | tf_op jit(solution)/shard_map/ppermute | solution.py:21
  17.7 1.3 fusion.33
  19.0 4.3 %fusion.47 = (f32[14,127,512]{2,0,1:T(8,128)}, f32[14,127,512]{2,0,1:T(8,128)}) fusion(f32[14,128,512]{2,0,1:T(8,128)S(1)} %copy.58), kind=kLoop, calls=%fused_computation.71 | loop fusion | bytes 14565376 | tf_op jit(solution)/shard_map/slice | solution.py:69
  23.6 1.5 copy.49
  25.1 1.4 copy.53
  26.5 21.7 %all-gather.1 = f32[1,1,4096]{2,0,1:T(1,128)S(1)} all-gather(f32[1,1,512]{2,0,1:T(1,128)S(1)} %slice.121), channel_id=3, replica_groups=mesh['grp'=4,'blk'=8] {'blk'}, dimensions={2}, use_global_device_ids=true | all-gather | bytes 18432 | tf_op jit(solution)/shard_map/all_gather | solution.py:59
  48.1 11.8 %gather_fusion.1 = f32[2048]{0:T(1024)S(1)} fusion(f32[4096]{0:T(1024)S(1)} %bitcast.52, s32[2048]{0:T(1024)S(1)} %broadcast_clamp_fusion), kind=kCustom, calls=%fused_computation.1 | custom fusion | bytes 24576 | tf_op jit(solution)/shard_map/jit(_take)/gather | solution.py:60
  59.9 24.8 %all-gather = f32[14,1,4096]{2,0,1:T(8,128)S(1)} all-gather(f32[14,1,512]{2,0,1:T(8,128)S(1)} %collective-permute-done), channel_id=2, replica_groups=mesh['grp'=4,'blk'=8] {'blk'}, dimensions={2}, use_global_device_ids=true | all-gather | bytes 258048 | tf_op jit(solution)/shard_map/all_gather | solution.py:53
  85.4 5.5 %gather_fusion = f32[2048,14]{1,0:T(8,128)S(1)} fusion(f32[14,4096]{0,1:T(8,128)S(1)} %copy.42, s32[2048]{0:T(1024)S(1)} %broadcast_clamp_fusion.1), kind=kCustom, calls=%fused_computation | custom fusion | bytes 237568 | tf_op jit(solution)/shard_map/jit(_take)/gather | solution.py:56
  92.7 0.8 fusion.38
  93.5 14.2 %fusion.19 = f32[14,128,512]{2,0,1:T(8,128)S(1)} fusion(f32[14,128,512]{2,0,1:T(8,128)} %copy-done.1, f32[14,128,1]{2,0,1:T(8,128)} %copy.53, f32[14,128,1]{2,0,1:T(8,128)} %copy.49, f32[14,1,512]{2,0,1:T(8,128)S(1)} %fusion.38, f32[14,127,512]{2,0,1:T(8,128)} %get-tuple-element.40, f32[14,127,512]{2,0,1:T(8,128)} %get-tuple-element.39, ...), kind=kOutput, calls=%fused_computation.24 | convolution fusion | flops 171573248 | bytes 15219528 | tf_op jit(solution)/shard_map/fg,gxr->fxr/dot_general | solution.py:31
  108.1 4.3 %fusion.44 = (f32[14,127,512]{2,0,1:T(8,128)}, f32[14,127,512]{2,0,1:T(8,128)}) fusion(f32[14,128,512]{2,0,1:T(8,128)S(1)} %fusion.19), kind=kLoop, calls=%fused_computation.68 | loop fusion | bytes 14565376 | tf_op jit(solution)/shard_map/slice | solution.py:69
  112.5 14.1 %collective-permute-start.4 = (f32[14,1,512]{2,0,1:T(8,128)S(1)}, f32[14,1,512]{2,0,1:T(8,128)S(1)}, u32[]{:S(2)}, u32[]{:S(2)}) collective-permute-start(f32[14,1,512]{2,0,1:T(8,128)S(1)} %get-tuple-element.29), channel_id=1, source_target_pairs={{0,8},{8,16},{16,24},{1,9},{9,17},{17,25},{2,10},{10,18},{18,26},{... | collective-permute-start | bytes 86024 | tf_op jit(solution)/shard_map/ppermute | solution.py:19
  127.3 3.2 %collective-permute-start.7 = (f32[14,128,1]{1,2,0:T(1,128)S(1)}, f32[14,128,1]{1,2,0:T(1,128)S(1)}, u32[]{:S(2)}, u32[]{:S(2)}) collective-permute-start(f32[14,128,1]{1,2,0:T(1,128)S(1)} %copy.61), channel_id=1, source_target_pairs={{1,0},{2,1},{3,2},{4,3},{5,4},{6,5},{7,6},{0,7},{9,8},{10,9},{11,1... | collective-permute-start | bytes 21512 | tf_op jit(solution)/shard_map/ppermute | solution.py:21
  130.5 2.9 %fusion.34 = f32[1,128,512]{2,0,1:T(1,128)S(1)} fusion(f32[14,128,512]{2,0,1:T(8,128)} %copy-done.2), kind=kLoop, calls=%fused_computation.43 | loop fusion | flops 458752 | bytes 524288 | tf_op jit(solution)/shard_map/add | solution.py:29
  133.4 2.1 %collective-permute-start.5 = (f32[14,1,512]{2,0,1:T(8,128)S(1)}, f32[14,1,512]{2,0,1:T(8,128)S(1)}, u32[]{:S(2)}, u32[]{:S(2)}) collective-permute-start(f32[14,1,512]{2,0,1:T(8,128)S(1)} %get-tuple-element.31), channel_id=1, source_target_pairs={{8,0},{16,8},{24,16},{9,1},{17,9},{25,17},{10,2},{18,10},{26,18},{... | collective-permute-start | bytes 86024 | tf_op jit(solution)/shard_map/ppermute | solution.py:21
  136.8 1.9 %collective-permute-done.5 = f32[14,1,512]{2,0,1:T(8,128)S(1)} collective-permute-done((f32[14,1,512]{2,0,1:T(8,128)S(1)}, f32[14,1,512]{2,0,1:T(8,128)S(1)}, u32[]{:S(2)}, u32[]{:S(2)}) %collective-permute-start.5) | collective-permute-done | bytes 28704 | tf_op jit(solution)/shard_map/ppermute | solution.py:21
  138.7 0.8 fusion.36
  139.4 16.4 %fusion.12 = f32[14,128,512]{2,0,1:T(8,128)S(1)} fusion(f32[14,128,1]{2,0,1:T(8,128)S(1)} %copy.62, f32[14,128,512]{2,0,1:T(8,128)} %copy-done.2, f32[14,128,1]{2,0,1:T(8,128)S(1)} %copy.60, f32[14,1,512]{2,0,1:T(8,128)S(1)} %fusion.36, f32[14,127,512]{2,0,1:T(8,128)} %get-tuple-element.33, f32[14,127,512]{2,0,1:T(8,128)} %get-tuple-element.32, ...), kind=kOutput, calls=%fused_computation.15 | convolution fusion | flops 173408256 | bytes 18889544 | tf_op jit(solution)/shard_map/fg,gxr->fxr/dot_general | solution.py:31
  155.8 4.0 %copy.63 = f32[14,128,512]{2,1,0:T(8,128)} copy(f32[14,128,512]{2,0,1:T(8,128)S(1)} %fusion.12) | data formatting | bytes 7340032 | tf_op jit(solution)/shard_map/mul | solution.py:84
  (55 shorter events, 5.6 us)
Async XLA Ops:
  0.0 93.5 %copy-start = (f32[14,14]{1,0:T(8,128)S(1)}, f32[14,14]{1,0:T(8,128)}, u32[]{:S(2)}) copy-start(f32[14,14]{1,0:T(8,128)} %param.14) | copy-start | bytes 2356
  2.1 22.9 %collective-permute-start.3 = (f32[14,128,1]{1,2,0:T(1,128)S(1)}, f32[14,128,1]{1,2,0:T(1,128)S(1)}, u32[]{:S(2)}, u32[]{:S(2)}) collective-permute-start(f32[14,128,1]{1,2,0:T(1,128)S(1)} %copy.67), channel_id=1, source_target_pairs={{1,0},{2,1},{3,2},{4,3},{5,4},{6,5},{7,6},{0,7},{9,8},{10,9},{11,1... | collective-permute-start | bytes 21512 | tf_op jit(solution)/shard_map/ppermute | solution.py:21
  7.5 16.0 %collective-permute-start.2 = (f32[14,128,1]{1,2,0:T(1,128)S(1)}, f32[14,128,1]{1,2,0:T(1,128)S(1)}, u32[]{:S(2)}, u32[]{:S(2)}) collective-permute-start(f32[14,128,1]{1,2,0:T(1,128)S(1)} %copy.66), channel_id=1, source_target_pairs={{0,1},{1,2},{2,3},{3,4},{4,5},{5,6},{6,7},{7,0},{8,9},{9,10},{10,1... | collective-permute-start | bytes 21512 | tf_op jit(solution)/shard_map/ppermute | solution.py:19
  11.7 11.6 %copy-start.1 = (f32[14,128,512]{2,0,1:T(8,128)}, f32[14,128,512]{2,0,1:T(8,128)S(1)}, u32[]{:S(2)}) copy-start(f32[14,128,512]{2,0,1:T(8,128)S(1)} %copy.58) | copy-start | bytes 11010052
  11.8 48.2 %collective-permute-start = (f32[14,1,512]{2,0,1:T(8,128)S(1)}, f32[14,1,512]{2,0,1:T(8,128)S(1)}, u32[]{:S(2)}, u32[]{:S(2)}) collective-permute-start(f32[14,1,512]{2,0,1:T(8,128)S(1)} %get-tuple-element.36), channel_id=1, source_target_pairs={{0,8},{8,16},{16,24},{1,9},{9,17},{17,25},{2,10},{10,18},{18,26},{... | collective-permute-start | bytes 86024 | tf_op jit(solution)/shard_map/ppermute | solution.py:19
  15.8 10.7 %collective-permute-start.1 = (f32[14,1,512]{2,0,1:T(8,128)S(1)}, f32[14,1,512]{2,0,1:T(8,128)S(1)}, u32[]{:S(2)}, u32[]{:S(2)}) collective-permute-start(f32[14,1,512]{2,0,1:T(8,128)S(1)} %get-tuple-element.38), channel_id=1, source_target_pairs={{8,0},{16,8},{24,16},{9,1},{17,9},{25,17},{10,2},{18,10},{26,18},{... | collective-permute-start | bytes 86024 | tf_op jit(solution)/shard_map/ppermute | solution.py:21
  19.0 4.4 %copy-start.3 = (s32[4,512]{1,0:T(4,128)S(1)}, s32[4,512]{1,0:T(4,128)}, u32[]{:S(2)}) copy-start(s32[4,512]{1,0:T(4,128)} %param.16) | copy-start | bytes 24580
  19.0 4.4 %copy-start.5 = (f32[4,512]{1,0:T(4,128)S(1)}, f32[4,512]{1,0:T(4,128)}, u32[]{:S(2)}) copy-start(f32[4,512]{1,0:T(4,128)} %param.17) | copy-start | bytes 24580
  19.0 4.4 %copy-start.4 = (s32[4,512]{1,0:T(4,128)S(1)}, s32[4,512]{1,0:T(4,128)}, u32[]{:S(2)}) copy-start(s32[4,512]{1,0:T(4,128)} %param.18) | copy-start | bytes 24580
  19.0 4.5 %copy-start.7 = (f32[14]{0:T(128)S(1)}, f32[14]{0:T(128)}, u32[]{:S(2)}) copy-start(f32[14]{0:T(128)} %param.15) | copy-start | bytes 172
  107.7 4.7 %copy-start.2 = (f32[14,128,512]{2,0,1:T(8,128)}, f32[14,128,512]{2,0,1:T(8,128)S(1)}, u32[]{:S(2)}) copy-start(f32[14,128,512]{2,0,1:T(8,128)S(1)} %fusion.19) | copy-start | bytes 11010052
  112.4 27.0 %copy-start.6 = (f32[128,512]{1,0:T(8,128)S(1)}, f32[128,512]{1,0:T(8,128)}, u32[]{:S(2)}) copy-start(f32[128,512]{1,0:T(8,128)} %param.13) | copy-start | bytes 786436
  112.5 24.3 %collective-permute-start.4 = (f32[14,1,512]{2,0,1:T(8,128)S(1)}, f32[14,1,512]{2,0,1:T(8,128)S(1)}, u32[]{:S(2)}, u32[]{:S(2)}) collective-permute-start(f32[14,1,512]{2,0,1:T(8,128)S(1)} %get-tuple-element.29), channel_id=1, source_target_pairs={{0,8},{8,16},{16,24},{1,9},{9,17},{17,25},{2,10},{10,18},{18,26},{... | collective-permute-start | bytes 86024 | tf_op jit(solution)/shard_map/ppermute | solution.py:19
  127.3 8.9 %collective-permute-start.7 = (f32[14,128,1]{1,2,0:T(1,128)S(1)}, f32[14,128,1]{1,2,0:T(1,128)S(1)}, u32[]{:S(2)}, u32[]{:S(2)}) collective-permute-start(f32[14,128,1]{1,2,0:T(1,128)S(1)} %copy.61), channel_id=1, source_target_pairs={{1,0},{2,1},{3,2},{4,3},{5,4},{6,5},{7,6},{0,7},{9,8},{10,9},{11,1... | collective-permute-start | bytes 21512 | tf_op jit(solution)/shard_map/ppermute | solution.py:21
  130.5 5.2 %collective-permute-start.6 = (f32[14,128,1]{1,2,0:T(1,128)S(1)}, f32[14,128,1]{1,2,0:T(1,128)S(1)}, u32[]{:S(2)}, u32[]{:S(2)}) collective-permute-start(f32[14,128,1]{1,2,0:T(1,128)S(1)} %copy.59), channel_id=1, source_target_pairs={{0,1},{1,2},{2,3},{3,4},{4,5},{5,6},{6,7},{7,0},{8,9},{9,10},{10,1... | collective-permute-start | bytes 21512 | tf_op jit(solution)/shard_map/ppermute | solution.py:19
  133.4 5.2 %collective-permute-start.5 = (f32[14,1,512]{2,0,1:T(8,128)S(1)}, f32[14,1,512]{2,0,1:T(8,128)S(1)}, u32[]{:S(2)}, u32[]{:S(2)}) collective-permute-start(f32[14,1,512]{2,0,1:T(8,128)S(1)} %get-tuple-element.31), channel_id=1, source_target_pairs={{8,0},{16,8},{24,16},{9,1},{17,9},{25,17},{10,2},{18,10},{26,18},{... | collective-permute-start | bytes 86024 | tf_op jit(solution)/shard_map/ppermute | solution.py:21
where the time goes:
time: 160 us
  blocking collectives  46.5 us (29%)
  local copies, waits for them, and re-layouts  42.7 us (27%)
  matrix products  30.6 us (19%)
  starting transfers between devices  30.4 us (19%)
  other arithmetic  7.22 us (5%)
  waiting for transfers between devices  1.97 us (1%)
    dot_general x2, matrix products, tendency(): jnp.einsum('fg,gxr->fxr', mix_matrix, reaction, precision=lax.Precision.H...  30.6 us
    all_gather x1, blocking collectives, shards(): donors = lax.all_gather(low_row, 'blk', axis=1, tiled=True)  24.8 us
    all_gather x1, blocking collectives, shards(): pressure = lax.all_gather(high_row[4], 'blk', axis=0, tiled=True)  21.7 us
    ppermute x4, starting transfers between devices, padded(): lax.ppermute(tail, axis, [(i, (i + 1) % count) for i in range(ends)])  18.1 us
    ppermute x4, starting transfers between devices, padded(): lax.ppermute(head, axis, [((i + 1) % count, i) for i in range(ends)])  12.3 us
    gather x2, local copies, waits for them, and re-layouts, shards(): jnp.take(pressure, outlet_ids) * outlet_weights  11.8 us
    slice x2, local copies, waits for them, and re-layouts, rate_of(): values[:, :-1, :]  8.64 us
    gather x1, local copies, waits for them, and re-layouts, shards(): picked = jnp.take(donors, jnp.clip(inlet_ids, 0, row_count - 1), axis=1)  5.48 us
  transfers between devices with their start and end apart: 8, of which 2 were waited for; matrix products, arithmetic and copies ran while one was open for 19% of the time, Pallas kernels for 0%

commit v1 on v0

--- a/solution.py
+++ b/solution.py
@@ -50,7 +50,15 @@
     axial_pad, cycle_pad = faces(fields)
     low_row = axial_pad[:, 0, :]
     high_row = axial_pad[:, -1, :]
-    donors = lax.all_gather(low_row, "blk", axis=1, tiled=True)
+    ways, here = (lax.axis_size("blk"), lax.axis_index("blk"))
+    grown, reach = (low_row, 1)
+    while reach < ways:
+        theirs = lax.ppermute(grown, "blk", [(d, d ^ reach) for d in range(ways)])
+        mine_first = jnp.concatenate([grown, theirs], axis=1)
+        theirs_first = jnp.concatenate([theirs, grown], axis=1)
+        grown = jnp.where(here & reach == 0, mine_first, theirs_first)
+        reach = 2 * reach
+    donors = grown
     row_count = donors.shape[1]
     inside = (inlet_ids >= 0) & (inlet_ids < row_count)
     picked = jnp.take(donors, jnp.clip(inlet_ids, 0, row_count - 1), axis=1)

time: 160 us -> 140 us (0.88)
  blocking collectives: 46.5 us -> 23.1 us
  waiting for transfers between devices: 1.97 us -> 9.83 us
  starting transfers between devices: 30.4 us -> 25.8 us
    all_gather x1 -> x0, blocking collectives: 24.8 us -> none  [shards(): donors = lax.all_gather(low_row, 'blk', axis=1, tiled=True)]
    ppermute x0 -> x3, waiting for transfers between devices: none -> 7.87 us  [shards(): theirs = lax.ppermute(grown, 'blk', [(d, d ^ reach) for d in range(ways)])]
    ppermute x4, starting transfers between devices: 18.1 us -> 15.6 us  [padded(): lax.ppermute(tail, axis, [(i, (i + 1) % count) for i in range(ends)])]
    ppermute x4, starting transfers between devices: 12.3 us -> 9.91 us  [padded(): lax.ppermute(head, axis, [((i + 1) % count, i) for i in range(ends)])]
    unnamed x23 -> x25, local copies, waits for them, and re-layouts: 4.88 us -> 4.88 us
  transfers between devices with their start and end apart: 8 -> 11, of which waited for: 2 -> 3; matrix products, arithmetic and copies ran while one was open for 19% -> 22% of each run, Pallas kernels for 0% -> 0%
where the time goes in v1:
time: 140 us
  local copies, waits for them, and re-layouts  42.7 us (30%)
  matrix products  31.1 us (22%)
  starting transfers between devices  25.8 us (18%)
  blocking collectives  23.1 us (16%)
  waiting for transfers between devices  9.83 us (7%)
  other arithmetic  6.56 us (5%)
    dot_general x2, matrix products, tendency(): jnp.einsum('fg,gxr->fxr', mix_matrix, reaction, precision=lax.Precision.H...  31.1 us
    all_gather x1, blocking collectives, shards(): pressure = lax.all_gather(high_row[4], 'blk', axis=0, tiled=True)  23.1 us
    ppermute x4, starting transfers between devices, padded(): lax.ppermute(tail, axis, [(i, (i + 1) % count) for i in range(ends)])  15.6 us
    gather x2, local copies, waits for them, and re-layouts, shards(): jnp.take(pressure, outlet_ids) * outlet_weights  11.8 us
    ppermute x4, starting transfers between devices, padded(): lax.ppermute(head, axis, [((i + 1) % count, i) for i in range(ends)])  9.91 us
    slice x2, local copies, waits for them, and re-layouts, rate_of(): values[:, :-1, :]  8.63 us
    ppermute x3, waiting for transfers between devices, shards(): theirs = lax.ppermute(grown, 'blk', [(d, d ^ reach) for d in range(ways)])  7.87 us
    gather x1, local copies, waits for them, and re-layouts, shards(): picked = jnp.take(donors, jnp.clip(inlet_ids, 0, row_count - 1), axis=1)  5.48 us
  transfers between devices with their start and end apart: 11, of which 3 were waited for; matrix products, arithmetic and copies ran while one was open for 22% of the time, Pallas kernels for 0%

profile of v1, /device:TPU:1, one launch (start us, length us, event | category | flops | bytes accessed | tf_op | source)
XLA Modules:
  0.0 139.6 jit_solution(6479627552937901393)
XLA Ops:
  0.0 1.8 %fusion.48 = (f32[14,128,1]{2,1,0:T(8,128)S(1)}, f32[14,128,1]{2,1,0:T(8,128)S(1)}) fusion(f32[14,128,512]{2,1,0:T(8,128)} %param.12), kind=kLoop, calls=%fused_computation.75 | loop fusion | bytes 28672 | tf_op jit(solution)/shard_map/slice | solution.py:16
  2.1 5.1 %collective-permute-start.6 = (f32[14,128,1]{1,2,0:T(1,128)S(1)}, f32[14,128,1]{1,2,0:T(1,128)S(1)}, u32[]{:S(2)}, u32[]{:S(2)}) collective-permute-start(f32[14,128,1]{1,2,0:T(1,128)S(1)} %copy.67), channel_id=1, source_target_pairs={{1,0},{2,1},{3,2},{4,3},{5,4},{6,5},{7,6},{0,7},{9,8},{10,9},{11,1... | collective-permute-start | bytes 21512 | tf_op jit(solution)/shard_map/ppermute | solution.py:21
  7.5 4.2 %copy.58 = f32[14,128,512]{2,0,1:T(8,128)S(1)} copy(f32[14,128,512]{2,1,0:T(8,128)} %param.12) | data formatting | bytes 7340032 | tf_op args[0]
  11.8 4.0 %collective-permute-start = (f32[14,1,512]{2,0,1:T(8,128)S(1)}, f32[14,1,512]{2,0,1:T(8,128)S(1)}, u32[]{:S(2)}, u32[]{:S(2)}) collective-permute-start(f32[14,1,512]{2,0,1:T(8,128)S(1)} %get-tuple-element.36), channel_id=1, source_target_pairs={{0,8},{8,16},{16,24},{1,9},{9,17},{17,25},{2,10},{10,18},{18,26},{... | collective-permute-start | bytes 86024 | tf_op jit(solution)/shard_map/ppermute | solution.py:19
  15.8 1.9 %collective-permute-start.4 = (f32[14,1,512]{2,0,1:T(8,128)S(1)}, f32[14,1,512]{2,0,1:T(8,128)S(1)}, u32[]{:S(2)}, u32[]{:S(2)}) collective-permute-start(f32[14,1,512]{2,0,1:T(8,128)S(1)} %get-tuple-element.38), channel_id=1, source_target_pairs={{8,0},{16,8},{24,16},{9,1},{17,9},{25,17},{10,2},{18,10},{26,18},{... | collective-permute-start | bytes 86024 | tf_op jit(solution)/shard_map/ppermute | solution.py:21
  17.7 1.3 fusion.33
  19.0 4.3 %fusion.47 = (f32[14,127,512]{2,0,1:T(8,128)}, f32[14,127,512]{2,0,1:T(8,128)}) fusion(f32[14,128,512]{2,0,1:T(8,128)S(1)} %copy.58), kind=kLoop, calls=%fused_computation.74 | loop fusion | bytes 14565376 | tf_op jit(solution)/shard_map/slice | solution.py:77
  23.7 1.5 %copy.49 = f32[14,128,1]{2,0,1:T(8,128)} copy(f32[14,128,1]{1,2,0:T(1,128)S(1)} %collective-permute-done.5) | data formatting | bytes 14336 | tf_op jit(solution)/shard_map/ppermute | solution.py:19
  25.1 1.4 %copy.53 = f32[14,128,1]{2,0,1:T(8,128)} copy(f32[14,128,1]{1,2,0:T(1,128)S(1)} %collective-permute-done.6) | data formatting | bytes 14336 | tf_op jit(solution)/shard_map/ppermute | solution.py:21
  26.6 23.1 %all-gather = f32[1,1,4096]{2,0,1:T(1,128)S(1)} all-gather(f32[1,1,512]{2,0,1:T(1,128)S(1)} %slice.121), channel_id=2, replica_groups=mesh['grp'=4,'blk'=8] {'blk'}, dimensions={2}, use_global_device_ids=true | all-gather | bytes 18432 | tf_op jit(solution)/shard_map/all_gather | solution.py:67
  49.7 11.8 %gather_fusion.1 = f32[2048]{0:T(1024)S(1)} fusion(f32[4096]{0:T(1024)S(1)} %bitcast.52, s32[2048]{0:T(1024)S(1)} %broadcast_clamp_fusion), kind=kCustom, calls=%fused_computation.1 | custom fusion | bytes 24576 | tf_op jit(solution)/shard_map/jit(_take)/gather | solution.py:68
  61.9 2.8 %collective-permute-done.2 = f32[14,1024]{1,0:T(8,128)S(1)} collective-permute-done((f32[14,1024]{1,0:T(8,128)S(1)}, f32[14,1024]{1,0:T(8,128)S(1)}, u32[]{:S(2)}, u32[]{:S(2)}) %collective-permute-start.2) | collective-permute-done | bytes 57376 | tf_op jit(solution)/shard_map/ppermute | solution.py:56
  64.8 0.8 fusion.38
  65.5 5.1 %collective-permute-done.3 = f32[14,2048]{1,0:T(8,128)S(1)} collective-permute-done((f32[14,2048]{1,0:T(8,128)S(1)}, f32[14,2048]{1,0:T(8,128)S(1)}, u32[]{:S(2)}, u32[]{:S(2)}) %collective-permute-start.3) | collective-permute-done | bytes 114720 | tf_op jit(solution)/shard_map/ppermute | solution.py:56
  71.3 5.5 %gather_fusion = f32[2048,14]{1,0:T(8,128)S(1)} fusion(f32[14,4096]{0,1:T(8,128)S(1)} %copy.42, s32[2048]{0:T(1024)S(1)} %broadcast_clamp_fusion.1), kind=kCustom, calls=%fused_computation | custom fusion | bytes 237568 | tf_op jit(solution)/shard_map/jit(_take)/gather | solution.py:64
  77.6 14.5 %fusion.19 = f32[14,128,512]{2,0,1:T(8,128)S(1)} fusion(f32[14,128,512]{2,0,1:T(8,128)} %copy-done.1, f32[14,128,1]{2,0,1:T(8,128)} %copy.53, f32[14,128,1]{2,0,1:T(8,128)} %copy.49, f32[14,1,512]{2,0,1:T(8,128)S(1)} %fusion.38, f32[14,127,512]{2,0,1:T(8,128)} %get-tuple-element.40, f32[14,127,512]{2,0,1:T(8,128)} %get-tuple-element.39, ...), kind=kOutput, calls=%fused_computation.24 | convolution fusion | flops 171573248 | bytes 15219528 | tf_op jit(solution)/shard_map/fg,gxr->fxr/dot_general | solution.py:31
  92.6 4.3 %fusion.44 = (f32[14,127,512]{2,0,1:T(8,128)}, f32[14,127,512]{2,0,1:T(8,128)}) fusion(f32[14,128,512]{2,0,1:T(8,128)S(1)} %fusion.19), kind=kLoop, calls=%fused_computation.71 | loop fusion | bytes 14565376 | tf_op jit(solution)/shard_map/slice | solution.py:77
  96.9 10.9 %collective-permute-start.7 = (f32[14,1,512]{2,0,1:T(8,128)S(1)}, f32[14,1,512]{2,0,1:T(8,128)S(1)}, u32[]{:S(2)}, u32[]{:S(2)}) collective-permute-start(f32[14,1,512]{2,0,1:T(8,128)S(1)} %get-tuple-element.29), channel_id=1, source_target_pairs={{0,8},{8,16},{16,24},{1,9},{9,17},{17,25},{2,10},{10,18},{18,26},{... | collective-permute-start | bytes 86024 | tf_op jit(solution)/shard_map/ppermute | solution.py:19
  110.0 2.9 %fusion.34 = f32[1,128,512]{2,0,1:T(1,128)S(1)} fusion(f32[14,128,512]{2,0,1:T(8,128)} %copy-done.2), kind=kLoop, calls=%fused_computation.43 | loop fusion | flops 458752 | bytes 524288 | tf_op jit(solution)/shard_map/add | solution.py:29
  113.0 2.1 %collective-permute-start.8 = (f32[14,1,512]{2,0,1:T(8,128)S(1)}, f32[14,1,512]{2,0,1:T(8,128)S(1)}, u32[]{:S(2)}, u32[]{:S(2)}) collective-permute-start(f32[14,1,512]{2,0,1:T(8,128)S(1)} %get-tuple-element.31), channel_id=1, source_target_pairs={{8,0},{16,8},{24,16},{9,1},{17,9},{25,17},{10,2},{18,10},{26,18},{... | collective-permute-start | bytes 86024 | tf_op jit(solution)/shard_map/ppermute | solution.py:21
  116.3 1.9 %collective-permute-done.8 = f32[14,1,512]{2,0,1:T(8,128)S(1)} collective-permute-done((f32[14,1,512]{2,0,1:T(8,128)S(1)}, f32[14,1,512]{2,0,1:T(8,128)S(1)}, u32[]{:S(2)}, u32[]{:S(2)}) %collective-permute-start.8) | collective-permute-done | bytes 28704 | tf_op jit(solution)/shard_map/ppermute | solution.py:21
  118.2 0.8 fusion.36
  119.0 16.6 %fusion.12 = f32[14,128,512]{2,0,1:T(8,128)S(1)} fusion(f32[14,128,1]{2,0,1:T(8,128)S(1)} %copy.62, f32[14,128,512]{2,0,1:T(8,128)} %copy-done.2, f32[14,128,1]{2,0,1:T(8,128)S(1)} %copy.60, f32[14,1,512]{2,0,1:T(8,128)S(1)} %fusion.36, f32[14,127,512]{2,0,1:T(8,128)} %get-tuple-element.33, f32[14,127,512]{2,0,1:T(8,128)} %get-tuple-element.32, ...), kind=kOutput, calls=%fused_computation.15 | convolution fusion | flops 173408256 | bytes 18889544 | tf_op jit(solution)/shard_map/fg,gxr->fxr/dot_general | solution.py:31
  135.6 4.0 %copy.63 = f32[14,128,512]{2,1,0:T(8,128)} copy(f32[14,128,512]{2,0,1:T(8,128)S(1)} %fusion.12) | data formatting | bytes 7340032 | tf_op jit(solution)/shard_map/mul | solution.py:92
  (65 shorter events, 6.6 us)
Async XLA Ops:
  0.0 77.6 %copy-start = (f32[14,14]{1,0:T(8,128)S(1)}, f32[14,14]{1,0:T(8,128)}, u32[]{:S(2)}) copy-start(f32[14,14]{1,0:T(8,128)} %param.14) | copy-start | bytes 2356
  2.1 23.0 %collective-permute-start.6 = (f32[14,128,1]{1,2,0:T(1,128)S(1)}, f32[14,128,1]{1,2,0:T(1,128)S(1)}, u32[]{:S(2)}, u32[]{:S(2)}) collective-permute-start(f32[14,128,1]{1,2,0:T(1,128)S(1)} %copy.67), channel_id=1, source_target_pairs={{1,0},{2,1},{3,2},{4,3},{5,4},{6,5},{7,6},{0,7},{9,8},{10,9},{11,1... | collective-permute-start | bytes 21512 | tf_op jit(solution)/shard_map/ppermute | solution.py:21
  7.5 16.1 %collective-permute-start.5 = (f32[14,128,1]{1,2,0:T(1,128)S(1)}, f32[14,128,1]{1,2,0:T(1,128)S(1)}, u32[]{:S(2)}, u32[]{:S(2)}) collective-permute-start(f32[14,128,1]{1,2,0:T(1,128)S(1)} %copy.66), channel_id=1, source_target_pairs={{0,1},{1,2},{2,3},{3,4},{4,5},{5,6},{6,7},{7,0},{8,9},{9,10},{10,1... | collective-permute-start | bytes 21512 | tf_op jit(solution)/shard_map/ppermute | solution.py:19
  11.7 11.6 %copy-start.1 = (f32[14,128,512]{2,0,1:T(8,128)}, f32[14,128,512]{2,0,1:T(8,128)S(1)}, u32[]{:S(2)}) copy-start(f32[14,128,512]{2,0,1:T(8,128)S(1)} %copy.58) | copy-start | bytes 11010052
  11.8 11.7 %collective-permute-start = (f32[14,1,512]{2,0,1:T(8,128)S(1)}, f32[14,1,512]{2,0,1:T(8,128)S(1)}, u32[]{:S(2)}, u32[]{:S(2)}) collective-permute-start(f32[14,1,512]{2,0,1:T(8,128)S(1)} %get-tuple-element.36), channel_id=1, source_target_pairs={{0,8},{8,16},{16,24},{1,9},{9,17},{17,25},{2,10},{10,18},{18,26},{... | collective-permute-start | bytes 86024 | tf_op jit(solution)/shard_map/ppermute | solution.py:19
  15.8 10.8 %collective-permute-start.4 = (f32[14,1,512]{2,0,1:T(8,128)S(1)}, f32[14,1,512]{2,0,1:T(8,128)S(1)}, u32[]{:S(2)}, u32[]{:S(2)}) collective-permute-start(f32[14,1,512]{2,0,1:T(8,128)S(1)} %get-tuple-element.38), channel_id=1, source_target_pairs={{8,0},{16,8},{24,16},{9,1},{17,9},{25,17},{10,2},{18,10},{26,18},{... | collective-permute-start | bytes 86024 | tf_op jit(solution)/shard_map/ppermute | solution.py:21
  19.0 4.4 %copy-start.3 = (s32[4,512]{1,0:T(4,128)S(1)}, s32[4,512]{1,0:T(4,128)}, u32[]{:S(2)}) copy-start(s32[4,512]{1,0:T(4,128)} %param.16) | copy-start | bytes 24580
  19.0 4.4 %copy-start.5 = (f32[4,512]{1,0:T(4,128)S(1)}, f32[4,512]{1,0:T(4,128)}, u32[]{:S(2)}) copy-start(f32[4,512]{1,0:T(4,128)} %param.17) | copy-start | bytes 24580
  19.0 4.4 %copy-start.4 = (s32[4,512]{1,0:T(4,128)S(1)}, s32[4,512]{1,0:T(4,128)}, u32[]{:S(2)}) copy-start(s32[4,512]{1,0:T(4,128)} %param.18) | copy-start | bytes 24580
  19.0 4.6 %copy-start.8 = (f32[14]{0:T(128)S(1)}, f32[14]{0:T(128)}, u32[]{:S(2)}) copy-start(f32[14]{0:T(128)} %param.15) | copy-start | bytes 172
  23.5 38.0 %collective-permute-start.1 = (f32[14,512]{1,0:T(8,128)S(1)}, f32[14,512]{1,0:T(8,128)S(1)}, u32[]{:S(2)}, u32[]{:S(2)}) collective-permute-start(f32[14,512]{1,0:T(8,128)S(1)} %bitcast.56), channel_id=1, source_target_pairs={{0,1},{1,0},{2,3},{3,2},{4,5},{5,4},{6,7},{7,6},{8,9},{9,8},{10,11... | collective-permute-start | bytes 86024 | tf_op jit(solution)/shard_map/ppermute | solution.py:56
  49.7 11.9 %copy-start.6 = (f32[4,512]{1,0:T(4,128)S(1)}, f32[4,512]{1,0:T(4,128)}, u32[]{:S(2)}) copy-start(f32[4,512]{1,0:T(4,128)} %param.19) | copy-start | bytes 24580
  61.5 3.2 %collective-permute-start.2 = (f32[14,1024]{1,0:T(8,128)S(1)}, f32[14,1024]{1,0:T(8,128)S(1)}, u32[]{:S(2)}, u32[]{:S(2)}) collective-permute-start(f32[14,1024]{1,0:T(8,128)S(1)} %maximum_select_fusion.2), channel_id=1, source_target_pairs={{0,2},{1,3},{2,0},{3,1},{4,6},{5,7},{6,4},{7,5},{8,10},{9,11},{10,... | collective-permute-start | bytes 172040 | tf_op jit(solution)/shard_map/ppermute | solution.py:56
  64.7 5.9 %collective-permute-start.3 = (f32[14,2048]{1,0:T(8,128)S(1)}, f32[14,2048]{1,0:T(8,128)S(1)}, u32[]{:S(2)}, u32[]{:S(2)}) collective-permute-start(f32[14,2048]{1,0:T(8,128)S(1)} %maximum_select_fusion.1), channel_id=1, source_target_pairs={{0,4},{1,5},{2,6},{3,7},{4,0},{5,1},{6,2},{7,3},{8,12},{9,13},{10,... | collective-permute-start | bytes 344072 | tf_op jit(solution)/shard_map/ppermute | solution.py:56
  92.1 4.7 %copy-start.2 = (f32[14,128,512]{2,0,1:T(8,128)}, f32[14,128,512]{2,0,1:T(8,128)S(1)}, u32[]{:S(2)}) copy-start(f32[14,128,512]{2,0,1:T(8,128)S(1)} %fusion.19) | copy-start | bytes 11010052
  96.9 22.1 %copy-start.7 = (f32[128,512]{1,0:T(8,128)S(1)}, f32[128,512]{1,0:T(8,128)}, u32[]{:S(2)}) copy-start(f32[128,512]{1,0:T(8,128)} %param.13) | copy-start | bytes 786436
  96.9 19.4 %collective-permute-start.7 = (f32[14,1,512]{2,0,1:T(8,128)S(1)}, f32[14,1,512]{2,0,1:T(8,128)S(1)}, u32[]{:S(2)}, u32[]{:S(2)}) collective-permute-start(f32[14,1,512]{2,0,1:T(8,128)S(1)} %get-tuple-element.29), channel_id=1, source_target_pairs={{0,8},{8,16},{16,24},{1,9},{9,17},{17,25},{2,10},{10,18},{18,26},{... | collective-permute-start | bytes 86024 | tf_op jit(solution)/shard_map/ppermute | solution.py:19
  108.6 7.2 %collective-permute-start.10 = (f32[14,128,1]{1,2,0:T(1,128)S(1)}, f32[14,128,1]{1,2,0:T(1,128)S(1)}, u32[]{:S(2)}, u32[]{:S(2)}) collective-permute-start(f32[14,128,1]{1,2,0:T(1,128)S(1)} %copy.61), channel_id=1, source_target_pairs={{1,0},{2,1},{3,2},{4,3},{5,4},{6,5},{7,6},{0,7},{9,8},{10,9},{11,1... | collective-permute-start | bytes 21512 | tf_op jit(solution)/shard_map/ppermute | solution.py:21
  109.3 5.9 %collective-permute-start.9 = (f32[14,128,1]{1,2,0:T(1,128)S(1)}, f32[14,128,1]{1,2,0:T(1,128)S(1)}, u32[]{:S(2)}, u32[]{:S(2)}) collective-permute-start(f32[14,128,1]{1,2,0:T(1,128)S(1)} %copy.59), channel_id=1, source_target_pairs={{0,1},{1,2},{2,3},{3,4},{4,5},{5,6},{6,7},{7,0},{8,9},{9,10},{10,1... | collective-permute-start | bytes 21512 | tf_op jit(solution)/shard_map/ppermute | solution.py:19
  113.0 5.2 %collective-permute-start.8 = (f32[14,1,512]{2,0,1:T(8,128)S(1)}, f32[14,1,512]{2,0,1:T(8,128)S(1)}, u32[]{:S(2)}, u32[]{:S(2)}) collective-permute-start(f32[14,1,512]{2,0,1:T(8,128)S(1)} %get-tuple-element.31), channel_id=1, source_target_pairs={{8,0},{16,8},{24,16},{9,1},{17,9},{25,17},{10,2},{18,10},{26,18},{... | collective-permute-start | bytes 86024 | tf_op jit(solution)/shard_map/ppermute | solution.py:21
